TPU v7x, 128 devices: a whole 4x4x4 slice. The times are simulated.
128 devices in a mesh: expert: 4 (over z_lo, core), fsdp: 32 (over y, z_hi, x).
Axes of the slice: x: 4, y: 4, z: 4 (z_hi: 2, z_lo: 2; z = z_hi * 2 + z_lo), core: 2. Of those that a mesh axis runs over, the one named last changes fastest.
Arguments:
- tokens: bfloat16 [16384, 2048], P(('expert', 'fsdp')), may hold values from -6 to 6
- expert_ids: int32 [16384, 1], P(('expert', 'fsdp')), may hold values from 0 to 7; in each aligned block of 128 rows (0 to 127, 128 to 255, ...) at most 24 rows name the same one
- gate_weight: bfloat16 [8, 2048, 8192], P('expert', None, 'fsdp'), may hold values from -0.125 to 0.125
- up_weight: bfloat16 [8, 2048, 8192], P('expert', None, 'fsdp'), may hold values from -0.125 to 0.125
- hidden_grad: bfloat16 [8, 3072, 8192], P('expert', None, 'fsdp'), may hold values from -0.1796875 to 0.1796875
Outputs:
- hidden: bfloat16 [8, 3072, 8192], P('expert', None, 'fsdp')
- gate_grad: float32 [8, 2048, 8192], P('expert', None, 'fsdp')
- up_grad: float32 [8, 2048, 8192], P('expert', None, 'fsdp')
Inputs may be any that keep to these rules, and one draw needn't show every extreme that they name: `expert_ids`: within the tokens of one device (aligned blocks of 128 rows) no expert is named more than 24 times, a bound that some block reaches.
All inputs are finite; a program needn't handle non-finite values.
Results may differ from a plain program's by a relative error of at most 0.003.
Values may be sent and summed in bfloat16 or wider, within the bound.
No kernel may reach another device: no remote copies, remote signals or barrier semaphores. Data moves between devices by JAX's collectives and lax.ppermute only.
A program may use at most 192 MiB of HBM per device.

v0:
```python
import jax
import jax.numpy as jnp
from jax import lax
from jax.sharding import PartitionSpec as P

CAP = 24


def make_fold(gate_part, up_part, grad_part, piece):
    groups, sources, count, model = piece.shape
    rows_flat = piece.reshape(groups, sources * count, model)
    gate = jnp.einsum("grd,gdf->grf", rows_flat, gate_part, preferred_element_type=jnp.float32)
    upval = jnp.einsum("grd,gdf->grf", rows_flat, up_part, preferred_element_type=jnp.float32)
    cotan = grad_part
    cotan = cotan.reshape(groups, sources * count, cotan.shape[3]).astype(jnp.float32)
    sigma = 1.0 / (1.0 + jnp.exp(-gate))
    active = gate * sigma
    hidden = (active * upval).astype(jnp.bfloat16)
    gate_delta = (cotan * upval * sigma * (1.0 + gate * (1.0 - sigma))).astype(jnp.bfloat16)
    up_delta = (cotan * active).astype(jnp.bfloat16)
    hidden_buf = hidden.reshape(groups, sources, count, hidden.shape[2])
    gate_sum = jnp.einsum("grd,grf->gdf", rows_flat, gate_delta, preferred_element_type=jnp.float32)
    up_sum = jnp.einsum("grd,grf->gdf", rows_flat, up_delta, preferred_element_type=jnp.float32)
    return (hidden_buf, gate_sum, up_sum)


def on_device(tokens, expert_ids, gate_weight, up_weight, hidden_grad):
    owners = lax.axis_size("expert")
    members = lax.axis_size("fsdp")
    per_owner = gate_weight.shape[0]
    model = gate_weight.shape[1]
    width = gate_weight.shape[2]
    route = expert_ids[:, 0]
    total_experts = per_owner * owners
    onehot = (route[:, None] == jnp.arange(total_experts, dtype=jnp.int32)[None, :]).astype(
        jnp.int32
    )
    rank = jnp.sum((jnp.cumsum(onehot, axis=0) - onehot) * onehot, axis=1)
    owner_of = route // per_owner
    within = route % per_owner
    target = within * (owners * CAP) + owner_of * CAP + rank
    send_rows = per_owner * owners * CAP
    placing = (jnp.arange(send_rows, dtype=jnp.int32)[:, None] == target[None, :]).astype(
        jnp.bfloat16
    )
    outgoing = jnp.dot(placing, tokens, preferred_element_type=jnp.float32).astype(jnp.bfloat16)
    outgoing = outgoing.reshape(per_owner, owners, CAP, model)
    slot_count = members * CAP
    grad_four = hidden_grad.reshape(per_owner, owners, slot_count, width)
    arrived = lax.all_to_all(outgoing, "expert", split_axis=1, concat_axis=1, tiled=True)
    hidden_buf, gate_sum, up_sum = make_fold(
        gate_weight, up_weight, grad_four, lax.all_gather(arrived, "fsdp", axis=2, tiled=True)
    )
    hidden = hidden_buf.reshape(per_owner, owners * slot_count, width)
    return (hidden, gate_sum, up_sum)


def solution(mesh):
    in_specs = (
        P(("expert", "fsdp"), None),
        P(("expert", "fsdp"), None),
        P("expert", None, "fsdp"),
        P("expert", None, "fsdp"),
        P("expert", None, "fsdp"),
    )
    out_specs = (P("expert", None, "fsdp"), P("expert", None, "fsdp"), P("expert", None, "fsdp"))
    return jax.shard_map(
        on_device, mesh=mesh, in_specs=in_specs, out_specs=out_specs, check_vma=False
    )
```

profile of v0, /device:TPU:24, one launch (start us, length us, event | category | flops | bytes accessed | tf_op | source)
XLA Modules:
  0.0 332.4 jit_solution(6977620930434274134)
XLA Ops:
  7.2 0.0 copy-start
  7.2 0.0 all-gather.2.cloned.1.call-start
  7.2 0.9 fusion.11
  8.1 0.2 reduce_window_sum.11
  8.3 0.8 select_reduce_fusion
  9.1 0.7 fusion.15
  9.8 1.4 convolution_convert_fusion
  11.2 0.1 copy.10
  11.3 14.8 %all_to_all.5 = bf16[2,4,24,2048]{3,2,0,1:T(8,128)(2,1)} all-to-all(bf16[2,4,24,2048]{3,2,0,1:T(8,128)(2,1)S(1)} %copy.10), channel_id=1, replica_groups=mesh['expert'=4,'fsdp'=32] {'expert'}, dimensions={1} | all-to-all | bytes 1572864 | tf_op jit(solution)/shard_map/all_to_all | solution.py:50
  26.0 0.0 all-gather.2.cloned.1.call-update
  26.1 210.8 %all-gather.2.cloned.1.call-done = bf16[2,4,768,2048]{3,2,0,1:T(8,128)(2,1)} async-done(((bf16[2,4,24,2048]{3,2,0,1:T(8,128)(2,1)}), bf16[2,4,768,2048]{3,2,0,1:T(8,128)(2,1)}) %all-gather.2.cloned.1.call-update) | async-done | bytes 25165840 | tf_op jit(solution)/shard_map/all_gather | solution.py:52
  236.8 0.0 copy-start.3
  236.8 21.2 %copy.11 = bf16[2,4,768,2048]{3,2,1,0:T(8,128)(2,1)} copy(bf16[2,4,768,2048]{3,2,0,1:T(8,128)(2,1)} %all-gather.2.cloned.1.call-done) | data formatting | bytes 50331648 | tf_op jit(solution)/shard_map/all_gather | solution.py:52
  258.0 0.0 copy-done.3
  258.0 0.0 copy-start.2
  258.0 14.5 %fusion.18 = f32[2,3072,256]{2,1,0:T(8,128)} fusion(bf16[2,3072,2048]{2,1,0:T(8,128)(2,1)} %bitcast.11, bf16[2,2048,256]{2,1,0:T(8,128)(2,1)S(1)} %copy-done.3), kind=kOutput, calls=%fused_computation.28 | convolution fusion | flops 6442450944 | bytes 33554432 | tf_op jit(solution)/shard_map/grd,gdf->grf/dot_general | solution.py:12
  272.5 0.0 copy-done.2
  272.5 17.5 %fusion.5 = f32[2,2048,256]{2,1,0:T(8,128)} fusion(bf16[2,3072,2048]{2,1,0:T(8,128)(2,1)} %bitcast.12, bf16[2,3072,256]{2,1,0:T(8,128)(2,1)S(1)} %copy-done.2, f32[2,3072,256]{2,1,0:T(8,128)} %fusion.18), kind=kOutput, calls=%fused_computation.9 | convolution fusion | flops 6453460992 | bytes 38797312 | tf_op jit(solution)/shard_map/grd,grf->gdf/dot_general | solution.py:23
  290.0 0.0 copy-done
  290.0 16.1 %multiply_convert_fusion = (bf16[2,3072,256]{2,1,0:T(8,128)(2,1)}, f32[2,3072,256]{2,1,0:T(8,128)}) fusion(f32[2,3072,256]{2,1,0:T(8,128)} %fusion.18, bf16[2,3072,2048]{2,1,0:T(8,128)(2,1)} %bitcast.13, bf16[2,2048,256]{2,1,0:T(8,128)(2,1)S(1)} %copy-done), kind=kOutput, calls=%fused_computation.6 | convolution fusion | flops 6451888128 | bytes 42991616 | tf_op jit(solution)/shard_map/grd,gdf->grf/dot_general | solution.py:13
  306.0 0.0 copy-start.1
  306.0 19.5 %fusion.7 = f32[2,2048,256]{2,1,0:T(8,128)} fusion(bf16[2,3072,2048]{2,1,0:T(8,128)(2,1)} %bitcast.14, f32[2,3072,256]{2,1,0:T(8,128)} %get-tuple-element.4, bf16[2,3072,256]{2,1,0:T(8,128)(2,1)S(1)} %copy-done.2, f32[2,3072,256]{2,1,0:T(8,128)} %fusion.18), kind=kOutput, calls=%fused_computation.10 | convolution fusion | flops 6459752448 | bytes 45088768 | tf_op jit(solution)/shard_map/grd,grf->gdf/dot_general | solution.py:22
  325.5 0.0 copy-done.1
Async XLA Ops:
  7.2 282.8 %copy-start = (bf16[2,2048,256]{2,1,0:T(8,128)(2,1)S(1)}, bf16[2,2048,256]{2,1,0:T(8,128)(2,1)}, u32[]{:S(2)}) copy-start(bf16[2,2048,256]{2,1,0:T(8,128)(2,1)} %param.8) | copy-start | bytes 6291460
  7.2 229.6 %all-gather.2.cloned.1.call-start = ((), (), s32[]{:S(2)}) async-start(), calls=%async_computation.1 | async-start | bytes 25952256 | tf_op jit(solution)/shard_map/all_gather | solution.py:52
  236.8 21.2 %copy-start.3 = (bf16[2,2048,256]{2,1,0:T(8,128)(2,1)S(1)}, bf16[2,2048,256]{2,1,0:T(8,128)(2,1)}, u32[]{:S(2)}) copy-start(bf16[2,2048,256]{2,1,0:T(8,128)(2,1)} %param.7) | copy-start | bytes 6291460
  258.0 14.5 %copy-start.2 = (bf16[2,3072,256]{2,1,0:T(8,128)(2,1)S(1)}, bf16[2,3072,256]{2,1,0:T(8,128)(2,1)}, u32[]{:S(2)}) copy-start(bf16[2,3072,256]{2,1,0:T(8,128)(2,1)} %param.9) | copy-start | bytes 9437188
  306.0 19.5 %copy-start.1 = (bf16[2,2048,256]{2,1,0:T(8,128)(2,1)S(1)}, bf16[2,2048,256]{2,1,0:T(8,128)(2,1)}, u32[]{:S(2)}) copy-start(bf16[2,2048,256]{2,1,0:T(8,128)(2,1)} %param.8) | copy-start | bytes 6291460
Sparse Core Ops, SparseCore 0:
  26.2 210.5 all-gather.1
where the time goes:
time: 334 us; the launch traced here: 332 us
  waiting for transfers between devices  211 us (63%)
  matrix products  68.9 us (21%)
  local copies, waits for them, and re-layouts  21.3 us (6%)
  blocking collectives  14.8 us (4%)
  between operations  14.1 us (4%)
    all_gather x1, waiting for transfers between devices, on_device(): lax.all_gather(arrived, 'fsdp', axis=2, tiled=True)  211 us
    all_gather x1, local copies, waits for them, and re-layouts, on_device(): lax.all_gather(arrived, 'fsdp', axis=2, tiled=True)  21.2 us
    dot_general x1, matrix products, make_fold(): jnp.einsum('grd,grf->gdf', rows_flat, gate_delta, preferred_element_type=...  19.5 us
    dot_general x1, matrix products, make_fold(): jnp.einsum('grd,grf->gdf', rows_flat, up_delta, preferred_element_type=jn...  17.5 us
    dot_general x1, matrix products, make_fold(): jnp.einsum('grd,gdf->grf', rows_flat, up_part, preferred_element_type=jnp...  16.1 us
    all_to_all x1, blocking collectives, on_device(): lax.all_to_all(outgoing, 'expert', split_axis=1, concat_axis=1, tiled=True)  14.8 us
    dot_general x1, matrix products, make_fold(): jnp.einsum('grd,gdf->grf', rows_flat, gate_part, preferred_element_type=j...  14.5 us
  transfers between devices with their start and end apart: 1, of which 1 were waited for; matrix products, arithmetic and copies ran while one was open for 0% of the time, Pallas kernels for 0%

commit v1 on v0

v1 whole, which is shorter than its diff:
```python
import jax
import jax.numpy as jnp
from jax import lax
from jax.sharding import PartitionSpec as P

CAP = 24


def chunk_pass(rows, gate_w, up_w, cotan):
    gate = jnp.einsum("grd,gdf->grf", rows, gate_w, preferred_element_type=jnp.float32)
    upval = jnp.einsum("grd,gdf->grf", rows, up_w, preferred_element_type=jnp.float32)
    cotan = cotan.astype(jnp.float32)
    sigma = 1.0 / (1.0 + jnp.exp(-gate))
    active = gate * sigma
    hidden = (active * upval).astype(jnp.bfloat16)
    gate_delta = (cotan * upval * sigma * (1.0 + gate * (1.0 - sigma))).astype(jnp.bfloat16)
    up_delta = (cotan * active).astype(jnp.bfloat16)
    gate_sum = jnp.einsum("grd,grf->gdf", rows, gate_delta, preferred_element_type=jnp.float32)
    up_sum = jnp.einsum("grd,grf->gdf", rows, up_delta, preferred_element_type=jnp.float32)
    return hidden, gate_sum, up_sum


def on_device(tokens, expert_ids, gate_weight, up_weight, hidden_grad):
    owners = lax.axis_size("expert")
    members = lax.axis_size("fsdp")
    per_owner = gate_weight.shape[0]
    model = gate_weight.shape[1]
    route = expert_ids[:, 0]
    total_experts = per_owner * owners
    onehot = (route[:, None] == jnp.arange(total_experts, dtype=jnp.int32)[None, :]).astype(
        jnp.int32
    )
    rank = jnp.sum((jnp.cumsum(onehot, axis=0) - onehot) * onehot, axis=1)
    owner_of = route // per_owner
    within = route % per_owner
    target = owner_of * (per_owner * CAP) + within * CAP + rank
    send_rows = per_owner * owners * CAP
    placing = (jnp.arange(send_rows, dtype=jnp.int32)[:, None] == target[None, :]).astype(
        jnp.bfloat16
    )
    outgoing = jnp.dot(placing, tokens, preferred_element_type=jnp.float32).astype(jnp.bfloat16)
    outgoing = outgoing.reshape(owners, per_owner, CAP, model)
    arrived = lax.all_to_all(outgoing, "expert", split_axis=0, concat_axis=0, tiled=True)
    slot_count = members * CAP

    def gather(source):
        piece = lax.dynamic_index_in_dim(arrived, source, axis=0, keepdims=False)
        return lax.all_gather(piece, "fsdp", axis=1, tiled=True)

    def step(source, rows, hidden_buf, gate_acc, up_acc):
        start = source * slot_count
        cotan = lax.dynamic_slice_in_dim(hidden_grad, start, slot_count, axis=1)
        hidden, gate_sum, up_sum = chunk_pass(rows, gate_weight, up_weight, cotan)
        hidden_buf = lax.dynamic_update_slice_in_dim(hidden_buf, hidden, start, axis=1)
        return hidden_buf, gate_acc + gate_sum, up_acc + up_sum

    def body(source, carry):
        rows, hidden_buf, gate_acc, up_acc = carry
        next_rows = gather(source + 1)
        hidden_buf, gate_acc, up_acc = step(source, rows, hidden_buf, gate_acc, up_acc)
        return next_rows, hidden_buf, gate_acc, up_acc

    hidden_buf = jnp.zeros(hidden_grad.shape, jnp.bfloat16)
    gate_acc = jnp.zeros(gate_weight.shape, jnp.float32)
    up_acc = jnp.zeros(up_weight.shape, jnp.float32)
    rows = gather(0)
    rows, hidden_buf, gate_acc, up_acc = lax.fori_loop(
        0, owners - 1, body, (rows, hidden_buf, gate_acc, up_acc)
    )
    hidden_buf, gate_acc, up_acc = step(owners - 1, rows, hidden_buf, gate_acc, up_acc)
    return (hidden_buf, gate_acc, up_acc)


def solution(mesh):
    in_specs = (
        P(("expert", "fsdp"), None),
        P(("expert", "fsdp"), None),
        P("expert", None, "fsdp"),
        P("expert", None, "fsdp"),
        P("expert", None, "fsdp"),
    )
    out_specs = (P("expert", None, "fsdp"), P("expert", None, "fsdp"), P("expert", None, "fsdp"))
    return jax.shard_map(
        on_device, mesh=mesh, in_specs=in_specs, out_specs=out_specs, check_vma=False
    )
```

time: 334 us -> 468 us (1.40)
  waiting for transfers between devices: 211 us -> 314 us
  local copies, waits for them, and re-layouts: 21.3 us -> 37.3 us
  matrix products: 68.9 us -> 84.5 us
    all_gather x1 -> x4, waiting for transfers between devices: 211 us -> 314 us  [gather(): return lax.all_gather(piece, 'fsdp', axis=1, tiled=True)]
    while x0 -> x29, local copies, waits for them, and re-layouts: none -> 32.1 us
    all_gather x1 -> x0, local copies, waits for them, and re-layouts: 21.2 us -> none  [on_device(): lax.all_gather(arrived, 'fsdp', axis=2, tiled=True)]
    dot_general x4 -> x16, matrix products: 67.5 us -> 84.1 us  [the longest x4 27.2 us: chunk_pass(): jnp.einsum('grd,grf->gdf', rows, gate_delta, preferred_element_type=jnp.f...]
  transfers between devices with their start and end apart: 1 -> 4, of which waited for: 1 -> 4; matrix products, arithmetic and copies ran while one was open for 0% -> 13% of each run, Pallas kernels for 0% -> 0%
where the time goes in v1:
time: 468 us; the launch traced here: 466 us
  waiting for transfers between devices  314 us (67%)
  matrix products  84.5 us (18%)
  local copies, waits for them, and re-layouts  37.3 us (8%)
  blocking collectives  14.6 us (3%)
  between operations  13.8 us (3%)
    all_gather x4, waiting for transfers between devices, gather(): return lax.all_gather(piece, 'fsdp', axis=1, tiled=True)  314 us
    dot_general x4, matrix products, chunk_pass(): jnp.einsum('grd,grf->gdf', rows, gate_delta, preferred_element_type=jnp.f...  27.2 us
    dot_general x4, matrix products, chunk_pass(): jnp.einsum('grd,grf->gdf', rows, up_delta, preferred_element_type=jnp.flo...  23.4 us
    dot_general x4, matrix products, chunk_pass(): jnp.einsum('grd,gdf->grf', rows, gate_w, preferred_element_type=jnp.float32)  21.4 us
    while x27, local copies, waits for them, and re-layouts  21 us
    all_to_all x1, blocking collectives, on_device(): lax.all_to_all(outgoing, 'expert', split_axis=0, concat_axis=0, tiled=True)  14.6 us
    dot_general x4, matrix products, chunk_pass(): jnp.einsum('grd,gdf->grf', rows, up_w, preferred_element_type=jnp.float32)  12.2 us
    while x2, local copies, waits for them, and re-layouts, on_device(): lax.fori_loop(0, owners - 1, body, (rows, hidden_buf, gate_acc, up_acc))  11 us
  transfers between devices with their start and end apart: 4, of which 4 were waited for; matrix products, arithmetic and copies ran while one was open for 13% of the time, Pallas kernels for 0%

profile of v1, /device:TPU:24, one launch (start us, length us, event | category | flops | bytes accessed | tf_op | source)
XLA Modules:
  0.0 466.5 jit_solution(2851810721346810936)
XLA Ops:
  7.2 0.0 copy-start
  7.2 0.0 all-gather.8.cloned.1.call-start
  7.2 0.8 fusion.28
  8.0 0.2 reduce_window_sum.11
  8.2 0.8 select_reduce_fusion
  9.0 0.7 fusion.32
  9.7 0.4 convolution_convert_fusion
  10.1 14.6 %all_to_all.5 = bf16[4,2,24,2048]{3,2,1,0:T(8,128)(2,1)S(1)} all-to-all(bf16[4,2,24,2048]{3,2,1,0:T(8,128)(2,1)S(1)} %bitcast.46), channel_id=1, replica_groups=mesh['expert'=4,'fsdp'=32] {'expert'}, dimensions={0} | all-to-all | bytes 1572864 | tf_op jit(solution)/shard_map/all_to_all | solution.py:43
  24.7 0.7 dynamic_slice.32
  25.4 0.0 all-gather.8.cloned.1.call-update
  25.4 94.2 %all-gather.8.cloned.1.call-done = bf16[1,2,768,2048]{3,2,1,0:T(8,128)(2,1)} async-done(((bf16[1,2,24,2048]{3,2,1,0:T(8,128)(2,1)}), bf16[1,2,768,2048]{3,2,1,0:T(8,128)(2,1)}) %all-gather.8.cloned.1.call-update) | async-done | bytes 6291472 | tf_op jit(solution)/shard_map/all_gather | solution.py:48
  119.7 1.9 broadcast_in_dim.2
  121.5 301.8 %while.22 = (s32[]{:T(128)}, bf16[2,768,2048]{2,1,0:T(8,128)(2,1)}, bf16[2,3072,256]{2,1,0:T(8,128)(2,1)}, f32[2,2048,256]{1,2,0:T(8,128)}, f32[2,2048,256]{1,2,...) while((s32[]{:T(128)}, bf16[2,768,2048]{2,1,0:T(8,128)(2,1)}, ...), condition=%wide.region_3.4_spmd.clone, body=%wide.region_2.3_spmd.clone.sunk | while | flops 6456082432 | bytes 130220424 | solution.py:67
  121.5 0.7 constant_dynamic-slice_fusion.2
  122.2 0.0 all-gather.10.cloned.1.call-update
  122.3 0.0 copy-start.5
  122.3 5.3 %fusion.68 = f32[2,768,256]{2,1,0:T(8,128)S(1)} fusion(bf16[2,768,2048]{2,1,0:T(8,128)(2,1)} %get-tuple-element.356, bf16[2,2048,256]{2,1,0:T(8,128)(2,1)} %get-tuple-element.375), kind=kOutput, calls=%fused_computation.51.clone.1 | convolution fusion | flops 1610612736 | bytes 9961472 | tf_op jit(solution)/shard_map/while/body/eval_jaxpr/grd,gdf->grf/dot_general | solution.py:10
  127.7 0.4 copy-done.5
  128.1 2.9 fusion.69
  131.0 4.1 bitcast_add_fusion.5
  135.1 4.4 bitcast_add_fusion.4
  139.5 76.2 %all-gather.10.cloned.1.call-done = bf16[1,2,768,2048]{3,2,1,0:T(8,128)(2,1)} async-done(((bf16[1,2,24,2048]{3,2,1,0:T(8,128)(2,1)}), bf16[1,2,768,2048]{3,2,1,0:T(8,128)(2,1)}) %all-gather.10.cloned.1.call-update) | async-done | bytes 6291472 | tf_op jit(solution)/shard_map/while/body/eval_jaxpr/all_gather | solution.py:48
  215.7 6.6 %copy.30 = bf16[2,768,2048]{2,1,0:T(8,128)(2,1)} copy(bf16[2,768,2048]{2,1,0:T(8,128)(2,1)} %bitcast.40) | data formatting | bytes 12582912 | tf_op jit(solution)/shard_map/while
  222.2 0.7 constant_dynamic-slice_fusion.2
  222.9 0.0 all-gather.10.cloned.1.call-update
  223.0 5.3 %fusion.68 = f32[2,768,256]{2,1,0:T(8,128)S(1)} fusion(bf16[2,768,2048]{2,1,0:T(8,128)(2,1)} %get-tuple-element.356, bf16[2,2048,256]{2,1,0:T(8,128)(2,1)} %get-tuple-element.375), kind=kOutput, calls=%fused_computation.51.clone.1 | convolution fusion | flops 1610612736 | bytes 9961472 | tf_op jit(solution)/shard_map/while/body/eval_jaxpr/grd,gdf->grf/dot_general | solution.py:10
  228.4 0.4 copy-done.5
  228.8 2.9 fusion.69
  231.7 6.3 %bitcast_add_fusion.5 = f32[2,2048,256]{1,2,0:T(8,128)} fusion(f32[2,2048,256]{1,2,0:T(8,128)} %get-tuple-element.359, bf16[2,768,2048]{2,1,0:T(8,128)(2,1)S(1)} %bitcast.43, pred[]{:T(512)S(6)} %compare.14, bf16[2,3072,256]{2,1,0:T(8,128)(2,1)S(1)} %copy-done.4, s32[]{:T(128)S(6)} %select_n.61, f32[2,768,256]{2,1,0:T(8,128)S(1)} %fusion.68), kind=kOutput, calls=%fused_computation.clone.1 | convolution fusion | flops 1615462400 | bytes 17039364 | tf_op jit(solution)/shard_map/while/body/eval_jaxpr/grd,grf->gdf/dot_general | solution.py:19
  238.0 6.6 %bitcast_add_fusion.4 = f32[2,2048,256]{1,2,0:T(8,128)} fusion(f32[2,2048,256]{1,2,0:T(8,128)} %get-tuple-element.358, bf16[2,768,2048]{2,1,0:T(8,128)(2,1)S(1)} %bitcast.43, pred[]{:T(512)S(6)} %compare.14, f32[2,768,256]{2,1,0:T(8,128)S(1)} %get-tuple-element.340, f32[2,768,256]{2,1,0:T(8,128)S(1)} %fusion.68, ...), kind=kOutput, calls=%fused_computation.1.clone.1 | convolution fusion | flops 1617035264 | bytes 18612228 | tf_op jit(solution)/shard_map/while/body/eval_jaxpr/grd,grf->gdf/dot_general | solution.py:18
  244.6 71.8 %all-gather.10.cloned.1.call-done = bf16[1,2,768,2048]{3,2,1,0:T(8,128)(2,1)} async-done(((bf16[1,2,24,2048]{3,2,1,0:T(8,128)(2,1)}), bf16[1,2,768,2048]{3,2,1,0:T(8,128)(2,1)}) %all-gather.10.cloned.1.call-update) | async-done | bytes 6291472 | tf_op jit(solution)/shard_map/while/body/eval_jaxpr/all_gather | solution.py:48
  316.4 6.6 %copy.30 = bf16[2,768,2048]{2,1,0:T(8,128)(2,1)} copy(bf16[2,768,2048]{2,1,0:T(8,128)(2,1)} %bitcast.40) | data formatting | bytes 12582912 | tf_op jit(solution)/shard_map/while
  322.9 0.7 constant_dynamic-slice_fusion.2
  323.6 0.0 all-gather.10.cloned.1.call-update
  323.7 5.3 %fusion.68 = f32[2,768,256]{2,1,0:T(8,128)S(1)} fusion(bf16[2,768,2048]{2,1,0:T(8,128)(2,1)} %get-tuple-element.356, bf16[2,2048,256]{2,1,0:T(8,128)(2,1)} %get-tuple-element.375), kind=kOutput, calls=%fused_computation.51.clone.1 | convolution fusion | flops 1610612736 | bytes 9961472 | tf_op jit(solution)/shard_map/while/body/eval_jaxpr/grd,gdf->grf/dot_general | solution.py:10
  329.1 0.4 copy-done.5
  329.5 2.9 fusion.69
  332.4 6.3 %bitcast_add_fusion.5 = f32[2,2048,256]{1,2,0:T(8,128)} fusion(f32[2,2048,256]{1,2,0:T(8,128)} %get-tuple-element.359, bf16[2,768,2048]{2,1,0:T(8,128)(2,1)S(1)} %bitcast.43, pred[]{:T(512)S(6)} %compare.14, bf16[2,3072,256]{2,1,0:T(8,128)(2,1)S(1)} %copy-done.4, s32[]{:T(128)S(6)} %select_n.61, f32[2,768,256]{2,1,0:T(8,128)S(1)} %fusion.68), kind=kOutput, calls=%fused_computation.clone.1 | convolution fusion | flops 1615462400 | bytes 17039364 | tf_op jit(solution)/shard_map/while/body/eval_jaxpr/grd,grf->gdf/dot_general | solution.py:19
  338.8 6.6 %bitcast_add_fusion.4 = f32[2,2048,256]{1,2,0:T(8,128)} fusion(f32[2,2048,256]{1,2,0:T(8,128)} %get-tuple-element.358, bf16[2,768,2048]{2,1,0:T(8,128)(2,1)S(1)} %bitcast.43, pred[]{:T(512)S(6)} %compare.14, f32[2,768,256]{2,1,0:T(8,128)S(1)} %get-tuple-element.340, f32[2,768,256]{2,1,0:T(8,128)S(1)} %fusion.68, ...), kind=kOutput, calls=%fused_computation.1.clone.1 | convolution fusion | flops 1617035264 | bytes 18612228 | tf_op jit(solution)/shard_map/while/body/eval_jaxpr/grd,grf->gdf/dot_general | solution.py:18
  345.3 71.4 %all-gather.10.cloned.1.call-done = bf16[1,2,768,2048]{3,2,1,0:T(8,128)(2,1)} async-done(((bf16[1,2,24,2048]{3,2,1,0:T(8,128)(2,1)}), bf16[1,2,768,2048]{3,2,1,0:T(8,128)(2,1)}) %all-gather.10.cloned.1.call-update) | async-done | bytes 6291472 | tf_op jit(solution)/shard_map/while/body/eval_jaxpr/all_gather | solution.py:48
  416.7 6.6 %copy.30 = bf16[2,768,2048]{2,1,0:T(8,128)(2,1)} copy(bf16[2,768,2048]{2,1,0:T(8,128)(2,1)} %bitcast.40) | data formatting | bytes 12582912 | tf_op jit(solution)/shard_map/while
  423.3 5.5 %copy.13 = f32[2,2048,256]{2,1,0:T(8,128)} copy(f32[2,2048,256]{1,2,0:T(8,128)} %get-tuple-element.229) | data formatting | bytes 8388608 | tf_op jit(solution)/shard_map/while | solution.py:67
  428.8 5.3 %fusion.36 = f32[2,768,256]{2,1,0:T(8,128)S(1)} fusion(bf16[2,768,2048]{2,1,0:T(8,128)(2,1)} %get-tuple-element.227, bf16[2,2048,256]{2,1,0:T(8,128)(2,1)} %get-tuple-element.392), kind=kOutput, calls=%fused_computation.52 | convolution fusion | flops 1610612736 | bytes 9961472 | tf_op jit(solution)/shard_map/grd,gdf->grf/dot_general | solution.py:10
  434.2 0.5 copy-done.1
  434.7 6.7 %convolution_add_fusion = f32[2,2048,256]{2,1,0:T(8,128)} fusion(f32[2,2048,256]{2,1,0:T(8,128)S(1)} %copy-done.1, bf16[2,768,2048]{2,1,0:T(8,128)(2,1)S(1)} %bitcast.45, bf16[2,3072,256]{2,1,0:T(8,128)(2,1)} %get-tuple-element.389, f32[2,768,256]{2,1,0:T(8,128)S(1)} %fusion.36), kind=kOutput, calls=%fused_computation.20 | convolution fusion | flops 1614413824 | bytes 17039360 | tf_op jit(solution)/shard_map/grd,grf->gdf/dot_general | solution.py:19
  441.4 3.4 fusion.21
  444.8 5.5 %copy.11 = f32[2,2048,256]{2,1,0:T(8,128)} copy(f32[2,2048,256]{1,2,0:T(8,128)} %get-tuple-element.228) | data formatting | bytes 8388608 | tf_op jit(solution)/shard_map/while | solution.py:67
  450.3 9.6 %convolution_add_fusion.1 = f32[2,2048,256]{2,1,0:T(8,128)} fusion(f32[2,2048,256]{2,1,0:T(8,128)} %copy.11, bf16[2,768,2048]{2,1,0:T(8,128)(2,1)} %get-tuple-element.227, f32[2,768,256]{2,1,0:T(8,128)} %get-tuple-element.281, f32[2,768,256]{2,1,0:T(8,128)S(1)} %copy-done.3, bf16[2,3072,256]{2,1,0:T(8,128)(2,1)} %get-tuple-element.389), kind=kOutput, calls=%fused_computation.21 | convolution fusion | flops 1615986688 | bytes 18612224 | tf_op jit(solution)/shard_map/grd,grf->gdf/dot_general | solution.py:18
  (41 shorter events, 0.1 us)
Async XLA Ops:
  7.2 2.5 copy-start
  7.2 112.5 %all-gather.8.cloned.1.call-start = ((), (), s32[]{:S(2)}) async-start(), calls=%async_computation.1 | async-start | bytes 6488064 | tf_op jit(solution)/shard_map/all_gather | solution.py:48
  121.5 94.1 %all-gather.10.cloned.1.call-start = ((), (), s32[]{:S(2)}) async-start(), calls=%async_computation.2 | async-start | bytes 6488064 | tf_op jit(solution)/shard_map/while/body/eval_jaxpr/all_gather | solution.py:48
  122.2 5.4 %slice-start = ((s8[6291456]{0:T(1024)(128)(4,1)}), s8[2097152]{0:T(1024)(128)(4,1)S(1)}, s32[]{:S(2)}) async-start(s8[6291456]{0:T(1024)(128)(4,1)} %bitcast.42), calls=%async_computation.3 | async-start | bytes 4194304 | tf_op jit(solution)/shard_map/while
  122.3 5.4 %slice-start.1 = ((s8[6291456]{0:T(1024)(128)(4,1)}), s8[4194304]{0:T(1024)(128)(4,1)S(1)}, s32[]{:S(2)}) async-start(s8[6291456]{0:T(1024)(128)(4,1)} %bitcast.42), calls=%async_computation.4 | async-start | bytes 8388608 | tf_op jit(solution)/shard_map/while
  122.3 5.8 %copy-start.5 = (bf16[2,2048,256]{2,1,0:T(8,128)(2,1)S(1)}, bf16[2,2048,256]{2,1,0:T(8,128)(2,1)}, u32[]{:S(2)}) copy-start(bf16[2,2048,256]{2,1,0:T(8,128)(2,1)} %get-tuple-element.376) | copy-start | bytes 6291460 | tf_op jit(solution)/shard_map/while
  128.1 2.9 copy-start.4
  222.2 94.1 %all-gather.10.cloned.1.call-start = ((), (), s32[]{:S(2)}) async-start(), calls=%async_computation.2 | async-start | bytes 6488064 | tf_op jit(solution)/shard_map/while/body/eval_jaxpr/all_gather | solution.py:48
  222.9 5.4 %slice-start = ((s8[6291456]{0:T(1024)(128)(4,1)}), s8[2097152]{0:T(1024)(128)(4,1)S(1)}, s32[]{:S(2)}) async-start(s8[6291456]{0:T(1024)(128)(4,1)} %bitcast.42), calls=%async_computation.3 | async-start | bytes 4194304 | tf_op jit(solution)/shard_map/while
  223.0 5.4 %slice-start.1 = ((s8[6291456]{0:T(1024)(128)(4,1)}), s8[4194304]{0:T(1024)(128)(4,1)S(1)}, s32[]{:S(2)}) async-start(s8[6291456]{0:T(1024)(128)(4,1)} %bitcast.42), calls=%async_computation.4 | async-start | bytes 8388608 | tf_op jit(solution)/shard_map/while
  223.0 5.8 %copy-start.5 = (bf16[2,2048,256]{2,1,0:T(8,128)(2,1)S(1)}, bf16[2,2048,256]{2,1,0:T(8,128)(2,1)}, u32[]{:S(2)}) copy-start(bf16[2,2048,256]{2,1,0:T(8,128)(2,1)} %get-tuple-element.376) | copy-start | bytes 6291460 | tf_op jit(solution)/shard_map/while
  228.8 2.9 copy-start.4
  322.9 93.8 %all-gather.10.cloned.1.call-start = ((), (), s32[]{:S(2)}) async-start(), calls=%async_computation.2 | async-start | bytes 6488064 | tf_op jit(solution)/shard_map/while/body/eval_jaxpr/all_gather | solution.py:48
  323.6 5.4 %slice-start = ((s8[6291456]{0:T(1024)(128)(4,1)}), s8[2097152]{0:T(1024)(128)(4,1)S(1)}, s32[]{:S(2)}) async-start(s8[6291456]{0:T(1024)(128)(4,1)} %bitcast.42), calls=%async_computation.3 | async-start | bytes 4194304 | tf_op jit(solution)/shard_map/while
  323.7 5.4 %slice-start.1 = ((s8[6291456]{0:T(1024)(128)(4,1)}), s8[4194304]{0:T(1024)(128)(4,1)S(1)}, s32[]{:S(2)}) async-start(s8[6291456]{0:T(1024)(128)(4,1)} %bitcast.42), calls=%async_computation.4 | async-start | bytes 8388608 | tf_op jit(solution)/shard_map/while
  323.7 5.8 %copy-start.5 = (bf16[2,2048,256]{2,1,0:T(8,128)(2,1)S(1)}, bf16[2,2048,256]{2,1,0:T(8,128)(2,1)}, u32[]{:S(2)}) copy-start(bf16[2,2048,256]{2,1,0:T(8,128)(2,1)} %get-tuple-element.376) | copy-start | bytes 6291460 | tf_op jit(solution)/shard_map/while
  329.5 2.9 copy-start.4
  423.3 10.9 %slice-start.2 = ((s8[6291456]{0:T(1024)(128)(4,1)}), s8[2097152]{0:T(1024)(128)(4,1)S(1)}, s32[]{:S(2)}) async-start(s8[6291456]{0:T(1024)(128)(4,1)} %bitcast.44), calls=%async_computation.5 | async-start | bytes 4194304
  428.8 5.4 %slice-start.3 = ((s8[6291456]{0:T(1024)(128)(4,1)}), s8[4194304]{0:T(1024)(128)(4,1)S(1)}, s32[]{:S(2)}) async-start(s8[6291456]{0:T(1024)(128)(4,1)} %bitcast.44), calls=%async_computation.6 | async-start | bytes 8388608
  428.8 5.9 %copy-start.1 = (f32[2,2048,256]{2,1,0:T(8,128)S(1)}, f32[2,2048,256]{2,1,0:T(8,128)}, u32[]{:S(2)}) copy-start(f32[2,2048,256]{2,1,0:T(8,128)} %copy.13) | copy-start | bytes 12582916
  434.7 6.7 %copy-start.2 = (f32[2,768,256]{2,1,0:T(8,128)}, f32[2,768,256]{2,1,0:T(8,128)S(1)}, u32[]{:S(2)}) copy-start(f32[2,768,256]{2,1,0:T(8,128)S(1)} %fusion.36) | copy-start | bytes 4718596
  434.7 6.7 %copy-start.6 = (bf16[2,2048,256]{2,1,0:T(8,128)(2,1)S(1)}, bf16[2,2048,256]{2,1,0:T(8,128)(2,1)}, u32[]{:S(2)}) copy-start(bf16[2,2048,256]{2,1,0:T(8,128)(2,1)} %get-tuple-element.393) | copy-start | bytes 6291460
  444.8 5.5 %copy-start.3 = (f32[2,768,256]{2,1,0:T(8,128)S(1)}, f32[2,768,256]{2,1,0:T(8,128)}, u32[]{:S(2)}) copy-start(f32[2,768,256]{2,1,0:T(8,128)} %copy-done.2) | copy-start | bytes 4718596
Sparse Core Ops, SparseCore 0:
  25.6 94.0 all-gather.7
  125.4 90.1 all-gather.9
  226.1 90.1 all-gather.9
  326.5 90.1 all-gather.9
